TPU v7x, 256 devices: a whole 4x4x8 slice. The times are simulated.
256 devices in a mesh: section: 4 (over x), seq: 16 (over z, y_hi), tp: 4 (over y_lo, core).
Axes of the slice: x: 4, y: 4 (y_hi: 2, y_lo: 2; y = y_hi * 2 + y_lo), z: 8, core: 2. Of those that a mesh axis runs over, the one named last changes fastest.
Arguments:
- queries: bfloat16 [4, 4096, 8192], P('section', 'seq', 'tp'), may hold values from -135 to 135
- upstream: bfloat16 [4, 4096, 8192], P('section', 'seq', 'tp'), may hold values from -48 to 48
- shared_kv: bfloat16 [2, 4096, 1024], P(None, ('seq', 'tp')), may hold values from -5 to 5
Outputs:
- d_queries: bfloat16 [4, 4096, 8192], P('section', 'seq', 'tp')
- d_shared_kv: float32 [2, 4096, 1024], P(None, ('seq', 'tp'))
All inputs are finite; a program needn't handle non-finite values.
Results may differ from a plain program's by a relative error of at most 0.0098.
Values may be sent and summed in bfloat16 or wider, within the bound.
No kernel may reach another device: no remote copies, remote signals or barrier semaphores. Data moves between devices by JAX's collectives and lax.ppermute only.
A program may use at most 128 MiB of HBM per device.

v0:
```python
import math
import jax
import jax.numpy as jnp
from jax import lax
from jax.sharding import PartitionSpec as P

QH = 64
KVH = 8
HD = 128
WINDOW = 1024


def shifted(value, axis, by):
    peers = lax.axis_size(axis)
    pairs = [(i, i + by) for i in range(peers) if 0 <= i + by < peers]
    return lax.ppermute(value, axis, pairs)


def head_grads(query_block, grad_block, keys_head, values_head, allowed, score_scale):
    scores = (
        jnp.einsum("rgd,ed->gre", query_block, keys_head, preferred_element_type=jnp.float32)
        * score_scale
    )
    masked = jnp.where(allowed[None], scores, -jnp.inf)
    highest = jnp.max(masked, axis=-1, keepdims=True)
    weights = jnp.exp(masked - highest)
    probs = weights / jnp.sum(weights, axis=-1, keepdims=True)
    probs_b = probs.astype(jnp.bfloat16)
    attn_out = jnp.einsum("gre,ed->rgd", probs_b, values_head, preferred_element_type=jnp.float32)
    delta = jnp.sum(grad_block.astype(jnp.float32) * attn_out, axis=-1)
    dprobs = jnp.einsum("rgd,ed->gre", grad_block, values_head, preferred_element_type=jnp.float32)
    dscores = probs * (dprobs - jnp.transpose(delta)[:, :, None])
    dscores_b = dscores.astype(jnp.bfloat16)
    grad_query = (
        jnp.einsum("gre,ed->rgd", dscores_b, keys_head, preferred_element_type=jnp.float32)
        * score_scale
    )
    grad_key = (
        jnp.einsum("gre,rgd->ed", dscores_b, query_block, preferred_element_type=jnp.float32)
        * score_scale
    )
    grad_value = jnp.einsum("gre,rgd->ed", probs_b, grad_block, preferred_element_type=jnp.float32)
    return (grad_query, grad_key, grad_value)


def body(queries, upstream, shared_kv):
    local_kv = lax.all_to_all(shared_kv, "tp", split_axis=2, concat_axis=1, tiled=True)
    tok_rows = local_kv.shape[1]
    kv_cols = local_kv.shape[2]
    head_size = HD
    local_kv_heads = kv_cols // head_size
    group_size = QH // KVH
    block_heads = max(1, group_size // 2)
    span_blocks = WINDOW // tok_rows
    score_scale = 1.0 / math.sqrt(head_size)
    earlier = [shifted(local_kv, "seq", span_blocks - offset) for offset in range(span_blocks)]
    extended = jnp.concatenate(earlier + [local_kv], axis=1)
    ext_rows = extended.shape[1]
    position = lax.axis_index("seq")
    row_ids = lax.broadcasted_iota(jnp.int32, (tok_rows, ext_rows), 0)
    key_ids = lax.broadcasted_iota(jnp.int32, (tok_rows, ext_rows), 1)
    allowed = (
        (key_ids >= row_ids + 1)
        & (key_ids <= row_ids + WINDOW)
        & (position * tok_rows - WINDOW + key_ids >= 0)
    )
    query_heads = queries.reshape(tok_rows, -1, head_size)
    grad_heads = upstream.reshape(tok_rows, -1, head_size)
    query_parts = []
    key_parts = []
    value_parts = []
    for kv_head in range(local_kv_heads):
        keys_head = extended[0, :, kv_head * head_size : (kv_head + 1) * head_size]
        values_head = extended[1, :, kv_head * head_size : (kv_head + 1) * head_size]
        key_total = jnp.zeros((ext_rows, head_size), jnp.float32)
        value_total = jnp.zeros((ext_rows, head_size), jnp.float32)
        for first_head in range(kv_head * group_size, (kv_head + 1) * group_size, block_heads):
            query_block = query_heads[:, first_head : first_head + block_heads]
            grad_block = grad_heads[:, first_head : first_head + block_heads]
            grad_query, grad_key, grad_value = head_grads(
                query_block, grad_block, keys_head, values_head, allowed, score_scale
            )
            query_parts.append(grad_query)
            key_total = key_total + grad_key
            value_total = value_total + grad_value
        key_parts.append(key_total)
        value_parts.append(value_total)
    d_queries = jnp.concatenate(query_parts, axis=1).reshape(1, tok_rows, -1).astype(jnp.bfloat16)
    grad_ext = jnp.stack([jnp.concatenate(key_parts, axis=1), jnp.concatenate(value_parts, axis=1)])
    own_rows = grad_ext[:, span_blocks * tok_rows :, :]
    for offset in range(span_blocks):
        own_rows = own_rows + shifted(
            grad_ext[:, offset * tok_rows : (offset + 1) * tok_rows, :].astype(jnp.bfloat16),
            "seq",
            offset - span_blocks,
        ).astype(jnp.float32)
    by_token = lax.all_to_all(own_rows, "tp", split_axis=1, concat_axis=2, tiled=True)
    sections = lax.axis_size("section")
    kinds, rows, cols = by_token.shape
    pieces = by_token.reshape(kinds, sections, rows // sections, cols)
    pieces = lax.all_to_all(pieces, "section", split_axis=1, concat_axis=1)
    chunk = pieces[:, 0]
    for other in range(1, sections):
        chunk = chunk + pieces[:, other]
    d_shared_kv = lax.all_gather(chunk, "section", axis=1, tiled=True)
    return (d_queries, d_shared_kv)


def solution(mesh):
    in_specs = (P("section", "seq", "tp"), P("section", "seq", "tp"), P(None, ("seq", "tp"), None))
    out_specs = (P("section", "seq", "tp"), P(None, ("seq", "tp"), None))
    return jax.shard_map(body, mesh=mesh, in_specs=in_specs, out_specs=out_specs, check_vma=False)
```

profile of v0, /device:TPU:80, one launch (start us, length us, event | category | flops | bytes accessed | tf_op | source)
XLA Modules:
  0.0 194.0 jit_solution(16692141543035240085)
XLA Ops:
  0.6 1.4 copy.93
  2.0 1.1 reshape.114
  3.1 3.4 %all-to-all-start = ((bf16[4,2,16384]{2,1,0:T(2,128)(2,1)}), bf16[4,2,16384]{2,1,0:T(2,128)(2,1)S(1)}, u32[]{:S(2)}, u32[]{:S(2)}) async-start(bf16[4,2,16384]{2,1,0:T(2,128)(2,1)} %reshape.114), calls=%async_computation | async-start | bytes 524288 | tf_op jit(solution)/shard_map/all_to_all | solution.py:47
  6.5 5.9 %all-to-all-done = bf16[4,2,16384]{2,1,0:T(2,128)(2,1)S(1)} async-done(((bf16[4,2,16384]{2,1,0:T(2,128)(2,1)}), bf16[4,2,16384]{2,1,0:T(2,128)(2,1)S(1)}, u32[]{:S(2)}, u32[]{:S(2)}) %all-to-all-start) | async-done | bytes 262176 | tf_op jit(solution)/shard_map/all_to_all | solution.py:47
  13.8 6.4 %collective-permute-start = (bf16[2,256,256]{2,1,0:T(8,128)(2,1)}, bf16[2,256,256]{2,1,0:T(8,128)(2,1)}, u32[]{:S(2)}, u32[]{:S(2)}) collective-permute-start(bf16[2,256,256]{2,1,0:T(8,128)(2,1)} %bitcast.2), channel_id=1, source_target_pairs={{0,16},{4,20},{8,24},{12,28},{16,32},{20,36},{24,40},{28,44},{32,4... | collective-permute-start | bytes 786440 | tf_op jit(solution)/shard_map/ppermute | solution.py:16
  20.2 1.1 fusion.28
  21.9 2.9 %collective-permute-start.2 = (bf16[2,256,256]{2,1,0:T(8,128)(2,1)}, bf16[2,256,256]{2,1,0:T(8,128)(2,1)}, u32[]{:S(2)}, u32[]{:S(2)}) collective-permute-start(bf16[2,256,256]{2,1,0:T(8,128)(2,1)} %bitcast.2), channel_id=1, source_target_pairs={{0,8},{4,12},{8,16},{12,20},{16,24},{20,28},{24,32},{28,36},{32,40... | collective-permute-start | bytes 786440 | tf_op jit(solution)/shard_map/ppermute | solution.py:16
  24.8 3.2 %collective-permute-start.1 = (bf16[2,256,256]{2,1,0:T(8,128)(2,1)}, bf16[2,256,256]{2,1,0:T(8,128)(2,1)}, u32[]{:S(2)}, u32[]{:S(2)}) collective-permute-start(bf16[2,256,256]{2,1,0:T(8,128)(2,1)} %bitcast.2), channel_id=1, source_target_pairs={{0,12},{4,16},{8,20},{12,24},{16,28},{20,32},{24,36},{28,40},{32,4... | collective-permute-start | bytes 786440 | tf_op jit(solution)/shard_map/ppermute | solution.py:16
  28.1 1.5 copy.95
  33.1 5.3 %collective-permute-start.3 = (bf16[2,256,256]{2,1,0:T(8,128)(2,1)}, bf16[2,256,256]{2,1,0:T(8,128)(2,1)S(1)}, u32[]{:S(2)}, u32[]{:S(2)}) collective-permute-start(bf16[2,256,256]{2,1,0:T(8,128)(2,1)} %bitcast.2), channel_id=1, source_target_pairs={{0,4},{4,8},{8,12},{12,16},{16,20},{20,24},{24,28},{28,32},{32,36}... | collective-permute-start | bytes 786440 | tf_op jit(solution)/shard_map/ppermute | solution.py:16
  39.4 10.3 %collective-permute-done.1 = bf16[2,256,256]{2,1,0:T(8,128)(2,1)} collective-permute-done((bf16[2,256,256]{2,1,0:T(8,128)(2,1)}, bf16[2,256,256]{2,1,0:T(8,128)(2,1)}, u32[]{:S(2)}, u32[]{:S(2)}) %collective-permute-start.1) | collective-permute-done | bytes 262176 | tf_op jit(solution)/shard_map/ppermute | solution.py:16
  51.6 2.3 %collective-permute-done.3 = bf16[2,256,256]{2,1,0:T(8,128)(2,1)S(1)} collective-permute-done((bf16[2,256,256]{2,1,0:T(8,128)(2,1)}, bf16[2,256,256]{2,1,0:T(8,128)(2,1)S(1)}, u32[]{:S(2)}, u32[]{:S(2)}) %collective-permute-start.3) | collective-permute-done | bytes 262176 | tf_op jit(solution)/shard_map/ppermute | solution.py:16
  54.9 5.3 %exponential_reduce_fusion.3 = (f32[4,256]{1,0:T(4,128)S(1)}, f32[4,256,1280]{1,2,0:T(8,128)}) fusion(pred[256,1280]{0,1:T(8,128)(4,1)} %fusion.28, bf16[256,16,128]{0,2,1:T(8,128)(2,1)S(1)} %bitcast.226, bf16[2,1280,256]{2,1,0:T(8,128)(2,1)S(1)} %constant_dynamic-update-slice_fusion), kind=kOutput, calls=%fused_computation.31 | convolution fusion | flops 340788480 | bytes 6164480 | tf_op jit(solution)/shard_map/sub | solution.py:26
  60.2 5.1 %exponential_reduce_fusion.1 = (f32[4,256]{1,0:T(4,128)S(1)}, f32[4,256,1280]{1,2,0:T(8,128)}) fusion(pred[256,1280]{0,1:T(8,128)(4,1)} %fusion.28, bf16[256,16,128]{0,2,1:T(8,128)(2,1)S(1)} %bitcast.227, bf16[2,1280,256]{2,1,0:T(8,128)(2,1)S(1)} %constant_dynamic-update-slice_fusion), kind=kOutput, calls=%fused_computation.27 | convolution fusion | flops 340788480 | bytes 6164480 | tf_op jit(solution)/shard_map/sub | solution.py:26
  65.3 5.1 %exponential_reduce_fusion.2 = (f32[4,256]{1,0:T(4,128)S(1)}, f32[4,256,1280]{1,2,0:T(8,128)}) fusion(pred[256,1280]{0,1:T(8,128)(4,1)} %fusion.28, bf16[256,16,128]{0,2,1:T(8,128)(2,1)S(1)} %bitcast.228, bf16[2,1280,256]{2,1,0:T(8,128)(2,1)S(1)} %constant_dynamic-update-slice_fusion), kind=kOutput, calls=%fused_computation.29 | convolution fusion | flops 340788480 | bytes 6164480 | tf_op jit(solution)/shard_map/sub | solution.py:26
  70.4 5.1 %exponential_reduce_fusion = (f32[4,256]{1,0:T(4,128)S(1)}, f32[4,256,1280]{1,2,0:T(8,128)}) fusion(pred[256,1280]{0,1:T(8,128)(4,1)} %fusion.28, bf16[256,16,128]{0,2,1:T(8,128)(2,1)S(1)} %bitcast.229, bf16[2,1280,256]{2,1,0:T(8,128)(2,1)S(1)} %constant_dynamic-update-slice_fusion), kind=kOutput, calls=%fused_computation.25 | convolution fusion | flops 340788480 | bytes 6164480 | tf_op jit(solution)/shard_map/sub | solution.py:26
  75.5 4.0 %fusion.23 = bf16[4,256,1280]{1,2,0:T(8,128)(2,1)S(1)} fusion(f32[4,256]{1,0:T(4,128)S(1)} %get-tuple-element.22, f32[4,256,1280]{1,2,0:T(8,128)} %get-tuple-element.23), kind=kLoop, calls=%fused_computation.50 | loop fusion | flops 2621440 | bytes 7868416 | tf_op jit(solution)/shard_map/convert_element_type | solution.py:28
  80.4 1.3 fusion.37
  81.8 1.1 fusion.15
  84.2 1.6 fusion.25
  86.9 1.3 fusion.39
  88.2 1.1 fusion.11
  91.6 1.4 fusion.24
  93.0 1.3 fusion.38
  95.3 1.1 fusion.13
  96.4 1.2 slice-done
  97.7 1.0 slice-done.1
  98.7 1.4 fusion.26
  100.2 1.3 fusion.40
  102.8 2.5 %fusion.9 = bf16[4,256,1280]{1,2,0:T(8,128)(2,1)S(1)} fusion(f32[4,256]{1,0:T(4,128)S(1)} %bitcast.239, f32[4,256]{1,0:T(4,128)S(1)} %get-tuple-element.16, f32[4,256,1280]{1,2,0:T(8,128)S(1)} %bitcast.219, bf16[2,1280,256]{2,1,0:T(8,128)(2,1)S(1)} %copy-done.5, bf16[256,16,128]{0,2,1:T(8,128)(2,1)} %bitcast.217), kind=kOutput, calls=%fused_computation.10 | convolution fusion | flops 340787200 | bytes 8462336 | tf_op jit(solution)/shard_map/rgd,ed->gre/dot_general | solution.py:31
  107.7 1.9 collective-permute-start.4
  109.6 3.8 %collective-permute-start.7 = (bf16[2,256,256]{1,2,0:T(8,128)(2,1)S(1)}, bf16[2,256,256]{1,2,0:T(8,128)(2,1)S(1)}, u32[]{:S(2)}, u32[]{:S(2)}) collective-permute-start(bf16[2,256,256]{1,2,0:T(8,128)(2,1)S(1)} %get-tuple-element.9), channel_id=1, source_target_pairs={{4,0},{8,4},{12,8},{16,12},{20,16},{24,20},{28,24},{32,28},{36,32}... | collective-permute-start | bytes 786440 | tf_op jit(solution)/shard_map/ppermute | solution.py:16
  113.4 1.9 collective-permute-start.6
  115.3 1.9 collective-permute-start.5
  117.8 8.0 %collective-permute-done.4 = bf16[2,256,256]{1,2,0:T(8,128)(2,1)S(1)} collective-permute-done((bf16[2,256,256]{1,2,0:T(8,128)(2,1)S(1)}, bf16[2,256,256]{1,2,0:T(8,128)(2,1)S(1)}, u32[]{:S(2)}, u32[]{:S(2)}) %collective-permute-start.4) | collective-permute-done | bytes 262176 | tf_op jit(solution)/shard_map/ppermute | solution.py:16
  125.8 7.0 %collective-permute-done.7 = bf16[2,256,256]{1,2,0:T(8,128)(2,1)S(1)} collective-permute-done((bf16[2,256,256]{1,2,0:T(8,128)(2,1)S(1)}, bf16[2,256,256]{1,2,0:T(8,128)(2,1)S(1)}, u32[]{:S(2)}, u32[]{:S(2)}) %collective-permute-start.7) | collective-permute-done | bytes 262176 | tf_op jit(solution)/shard_map/ppermute | solution.py:16
  132.8 17.3 %collective-permute-done.5 = bf16[2,256,256]{1,2,0:T(8,128)(2,1)S(1)} collective-permute-done((bf16[2,256,256]{1,2,0:T(8,128)(2,1)S(1)}, bf16[2,256,256]{1,2,0:T(8,128)(2,1)S(1)}, u32[]{:S(2)}, u32[]{:S(2)}) %collective-permute-start.5) | collective-permute-done | bytes 262176 | tf_op jit(solution)/shard_map/ppermute | solution.py:16
  151.3 3.5 %all-to-all-start.1 = ((f32[2,256,256]{2,0,1:T(2,128)}), f32[2,256,256]{2,0,1:T(2,128)S(1)}, u32[]{:S(2)}, u32[]{:S(2)}) async-start(f32[2,256,256]{2,0,1:T(2,128)} %copy.141), calls=%async_computation.1 | async-start | bytes 1048576 | tf_op jit(solution)/shard_map/all_to_all | solution.py:97
  154.8 3.2 %fusion.42 = bf16[256,4,128]{0,2,1:T(8,128)(2,1)} fusion(bf16[4,256,1280]{1,2,0:T(8,128)(2,1)} %copy-done.2, bf16[2,1280,256]{2,1,0:T(8,128)(2,1)} %copy-done.4), kind=kOutput, calls=%fused_computation.81 | convolution fusion | flops 335806464 | bytes 3211264 | tf_op jit(solution)/shard_map/gre,ed->rgd/dot_general | solution.py:35
  158.0 2.2 %fusion.43 = bf16[256,4,128]{0,2,1:T(8,128)(2,1)} fusion(bf16[4,256,1280]{1,2,0:T(8,128)(2,1)S(1)} %copy-done.1, bf16[2,1280,256]{2,1,0:T(8,128)(2,1)} %copy-done.4), kind=kOutput, calls=%fused_computation.82 | convolution fusion | flops 335806464 | bytes 3211264 | tf_op jit(solution)/shard_map/gre,ed->rgd/dot_general | solution.py:35
  160.2 3.3 %all-to-all-done.1 = f32[2,256,256]{2,0,1:T(2,128)S(1)} async-done(((f32[2,256,256]{2,0,1:T(2,128)}), f32[2,256,256]{2,0,1:T(2,128)S(1)}, u32[]{:S(2)}, u32[]{:S(2)}) %all-to-all-start.1) | async-done | bytes 524320 | tf_op jit(solution)/shard_map/all_to_all | solution.py:97
  163.9 1.1 reshape.92
  165.0 1.9 copy.144
  166.9 4.3 %all-to-all-start.2 = ((f32[2,4,16,1024]{3,2,0,1:T(8,128)}), f32[2,4,16,1024]{3,2,0,1:T(8,128)S(1)}, u32[]{:S(2)}, u32[]{:S(2)}) async-start(f32[2,4,16,1024]{3,2,0,1:T(8,128)} %copy.144), calls=%async_computation.2 | async-start | bytes 1048576 | tf_op jit(solution)/shard_map/all_to_all | solution.py:101
  171.2 1.6 fusion.41
  172.9 1.4 copy.145
  174.3 6.0 %all-to-all-done.2 = f32[2,4,16,1024]{3,2,0,1:T(8,128)S(1)} async-done(((f32[2,4,16,1024]{3,2,0,1:T(8,128)}), f32[2,4,16,1024]{3,2,0,1:T(8,128)S(1)}, u32[]{:S(2)}, u32[]{:S(2)}) %all-to-all-start.2) | async-done | bytes 524320 | tf_op jit(solution)/shard_map/all_to_all | solution.py:101
  180.4 12.8 %all-gather = f32[2,1,64,1024]{3,2,0,1:T(8,128)S(1)} all-gather(f32[2,1,16,1024]{3,2,0,1:T(8,128)S(1)} %slice_add_fusion), channel_id=2, replica_groups=mesh['section'=4,'seq'=16,'tp'=4] {'section'}, dimensions={2}, use_global_device_ids=true | all-gather | bytes 655360 | tf_op jit(solution)/shard_map/all_gather | solution.py:105
  (86 shorter events, 22.7 us)
Async XLA Ops:
  0.6 20.7 %copy-start.12 = (bf16[1,256,2048]{2,1,0:T(8,128)(2,1)S(1)}, bf16[1,256,2048]{2,1,0:T(8,128)(2,1)}, u32[]{:S(2)}) copy-start(bf16[1,256,2048]{2,1,0:T(8,128)(2,1)} %param.4) | copy-start | bytes 3145732
  3.1 9.4 %all-to-all-start = ((bf16[4,2,16384]{2,1,0:T(2,128)(2,1)}), bf16[4,2,16384]{2,1,0:T(2,128)(2,1)S(1)}, u32[]{:S(2)}, u32[]{:S(2)}) async-start(bf16[4,2,16384]{2,1,0:T(2,128)(2,1)} %reshape.114), calls=%async_computation | async-start | bytes 524288 | tf_op jit(solution)/shard_map/all_to_all | solution.py:47
  13.8 24.6 %collective-permute-start = (bf16[2,256,256]{2,1,0:T(8,128)(2,1)}, bf16[2,256,256]{2,1,0:T(8,128)(2,1)}, u32[]{:S(2)}, u32[]{:S(2)}) collective-permute-start(bf16[2,256,256]{2,1,0:T(8,128)(2,1)} %bitcast.2), channel_id=1, source_target_pairs={{0,16},{4,20},{8,24},{12,28},{16,32},{20,36},{24,40},{28,44},{32,4... | collective-permute-start | bytes 786440 | tf_op jit(solution)/shard_map/ppermute | solution.py:16
  21.9 79.6 %copy-start.3 = (bf16[1,256,2048]{1,2,0:T(8,128)(2,1)}, bf16[1,256,2048]{1,2,0:T(8,128)(2,1)S(1)}, u32[]{:S(2)}) copy-start(bf16[1,256,2048]{1,2,0:T(8,128)(2,1)S(1)} %copy.97) | copy-start | bytes 3145732
  21.9 28.7 %collective-permute-start.2 = (bf16[2,256,256]{2,1,0:T(8,128)(2,1)}, bf16[2,256,256]{2,1,0:T(8,128)(2,1)}, u32[]{:S(2)}, u32[]{:S(2)}) collective-permute-start(bf16[2,256,256]{2,1,0:T(8,128)(2,1)} %bitcast.2), channel_id=1, source_target_pairs={{0,8},{4,12},{8,16},{12,20},{16,24},{20,28},{24,32},{28,36},{32,40... | collective-permute-start | bytes 786440 | tf_op jit(solution)/shard_map/ppermute | solution.py:16
  24.8 24.8 %collective-permute-start.1 = (bf16[2,256,256]{2,1,0:T(8,128)(2,1)}, bf16[2,256,256]{2,1,0:T(8,128)(2,1)}, u32[]{:S(2)}, u32[]{:S(2)}) collective-permute-start(bf16[2,256,256]{2,1,0:T(8,128)(2,1)} %bitcast.2), channel_id=1, source_target_pairs={{0,12},{4,16},{8,20},{12,24},{16,28},{20,32},{24,36},{28,40},{32,4... | collective-permute-start | bytes 786440 | tf_op jit(solution)/shard_map/ppermute | solution.py:16
  29.6 59.7 %copy-start.6 = (bf16[1,256,2048]{1,2,0:T(8,128)(2,1)}, bf16[1,256,2048]{1,2,0:T(8,128)(2,1)S(1)}, u32[]{:S(2)}) copy-start(bf16[1,256,2048]{1,2,0:T(8,128)(2,1)S(1)} %copy.95) | copy-start | bytes 3145732
  33.1 20.8 %collective-permute-start.3 = (bf16[2,256,256]{2,1,0:T(8,128)(2,1)}, bf16[2,256,256]{2,1,0:T(8,128)(2,1)S(1)}, u32[]{:S(2)}, u32[]{:S(2)}) collective-permute-start(bf16[2,256,256]{2,1,0:T(8,128)(2,1)} %bitcast.2), channel_id=1, source_target_pairs={{0,4},{4,8},{8,12},{12,16},{16,20},{20,24},{24,28},{28,32},{32,36}... | collective-permute-start | bytes 786440 | tf_op jit(solution)/shard_map/ppermute | solution.py:16
  54.9 45.3 %copy-start.4 = (bf16[2,1280,256]{2,1,0:T(8,128)(2,1)}, bf16[2,1280,256]{2,1,0:T(8,128)(2,1)S(1)}, u32[]{:S(2)}) copy-start(bf16[2,1280,256]{2,1,0:T(8,128)(2,1)S(1)} %constant_dynamic-update-slice_fusion) | copy-start | bytes 3932164
  75.5 6.3 %slice-start.6 = ((s8[5242880]{0:T(1024)(128)(4,1)}), s8[4194304]{0:T(1024)(128)(4,1)S(1)}, s32[]{:S(2)}) async-start(s8[5242880]{0:T(1024)(128)(4,1)} %bitcast.224), calls=%async_computation.9 | async-start | bytes 8388608
  79.4 1.0 copy-start.11
  79.5 2.3 %slice-start.7 = ((s8[5242880]{0:T(1024)(128)(4,1)}), s8[1048576]{0:T(1024)(128)(4,1)S(1)}, s32[]{:S(2)}) async-start(s8[5242880]{0:T(1024)(128)(4,1)} %bitcast.224), calls=%async_computation.10 | async-start | bytes 2097152
  81.7 2.2 %slice-start.4 = ((s8[5242880]{0:T(1024)(128)(4,1)}), s8[4194304]{0:T(1024)(128)(4,1)S(1)}, s32[]{:S(2)}) async-start(s8[5242880]{0:T(1024)(128)(4,1)} %bitcast.222), calls=%async_computation.7 | async-start | bytes 8388608
  81.8 2.5 %slice-start.5 = ((s8[5242880]{0:T(1024)(128)(4,1)}), s8[1048576]{0:T(1024)(128)(4,1)S(1)}, s32[]{:S(2)}) async-start(s8[5242880]{0:T(1024)(128)(4,1)} %bitcast.222), calls=%async_computation.8 | async-start | bytes 2097152
  85.9 1.0 copy-start.10
  88.1 2.7 %slice-start.2 = ((s8[5242880]{0:T(1024)(128)(4,1)}), s8[4194304]{0:T(1024)(128)(4,1)S(1)}, s32[]{:S(2)}) async-start(s8[5242880]{0:T(1024)(128)(4,1)} %bitcast.220), calls=%async_computation.5 | async-start | bytes 8388608
  88.1 3.4 %slice-start.3 = ((s8[5242880]{0:T(1024)(128)(4,1)}), s8[1048576]{0:T(1024)(128)(4,1)S(1)}, s32[]{:S(2)}) async-start(s8[5242880]{0:T(1024)(128)(4,1)} %bitcast.220), calls=%async_computation.6 | async-start | bytes 2097152
  89.3 1.6 copy-start.2
  91.6 1.4 copy-start.9
  95.3 2.4 %slice-start = ((s8[5242880]{0:T(1024)(128)(4,1)}), s8[4194304]{0:T(1024)(128)(4,1)S(1)}, s32[]{:S(2)}) async-start(s8[5242880]{0:T(1024)(128)(4,1)} %bitcast.218), calls=%async_computation.3 | async-start | bytes 8388608
  95.3 3.4 %slice-start.1 = ((s8[5242880]{0:T(1024)(128)(4,1)}), s8[1048576]{0:T(1024)(128)(4,1)S(1)}, s32[]{:S(2)}) async-start(s8[5242880]{0:T(1024)(128)(4,1)} %bitcast.218), calls=%async_computation.4 | async-start | bytes 2097152
  96.4 8.8 %copy-start = (bf16[4,256,1280]{1,2,0:T(8,128)(2,1)}, bf16[4,256,1280]{1,2,0:T(8,128)(2,1)S(1)}, u32[]{:S(2)}) copy-start(bf16[4,256,1280]{1,2,0:T(8,128)(2,1)S(1)} %fusion.13) | copy-start | bytes 7864324
  98.7 1.4 copy-start.8
  101.4 1.3 copy-start.5
  102.8 2.5 %copy-start.7 = (bf16[1,256,2048]{1,2,0:T(8,128)(2,1)S(1)}, bf16[1,256,2048]{1,2,0:T(8,128)(2,1)}, u32[]{:S(2)}) copy-start(bf16[1,256,2048]{1,2,0:T(8,128)(2,1)} %copy-done.6) | copy-start | bytes 3145732
  107.7 18.1 %collective-permute-start.4 = (bf16[2,256,256]{1,2,0:T(8,128)(2,1)S(1)}, bf16[2,256,256]{1,2,0:T(8,128)(2,1)S(1)}, u32[]{:S(2)}, u32[]{:S(2)}) collective-permute-start(bf16[2,256,256]{1,2,0:T(8,128)(2,1)S(1)} %get-tuple-element.8), channel_id=1, source_target_pairs={{16,0},{20,4},{24,8},{28,12},{32,16},{36,20},{40,24},{44,28},{48,3... | collective-permute-start | bytes 786440 | tf_op jit(solution)/shard_map/ppermute | solution.py:16
  109.6 23.2 %collective-permute-start.7 = (bf16[2,256,256]{1,2,0:T(8,128)(2,1)S(1)}, bf16[2,256,256]{1,2,0:T(8,128)(2,1)S(1)}, u32[]{:S(2)}, u32[]{:S(2)}) collective-permute-start(bf16[2,256,256]{1,2,0:T(8,128)(2,1)S(1)} %get-tuple-element.9), channel_id=1, source_target_pairs={{4,0},{8,4},{12,8},{16,12},{20,16},{24,20},{28,24},{32,28},{36,32}... | collective-permute-start | bytes 786440 | tf_op jit(solution)/shard_map/ppermute | solution.py:16
  113.4 19.4 %collective-permute-start.6 = (bf16[2,256,256]{1,2,0:T(8,128)(2,1)S(1)}, bf16[2,256,256]{1,2,0:T(8,128)(2,1)S(1)}, u32[]{:S(2)}, u32[]{:S(2)}) collective-permute-start(bf16[2,256,256]{1,2,0:T(8,128)(2,1)S(1)} %get-tuple-element.10), channel_id=1, source_target_pairs={{8,0},{12,4},{16,8},{20,12},{24,16},{28,20},{32,24},{36,28},{40,32... | collective-permute-start | bytes 786440 | tf_op jit(solution)/shard_map/ppermute | solution.py:16
  115.3 34.8 %collective-permute-start.5 = (bf16[2,256,256]{1,2,0:T(8,128)(2,1)S(1)}, bf16[2,256,256]{1,2,0:T(8,128)(2,1)S(1)}, u32[]{:S(2)}, u32[]{:S(2)}) collective-permute-start(bf16[2,256,256]{1,2,0:T(8,128)(2,1)S(1)} %get-tuple-element.11), channel_id=1, source_target_pairs={{12,0},{16,4},{20,8},{24,12},{28,16},{32,20},{36,24},{40,28},{44,3... | collective-permute-start | bytes 786440 | tf_op jit(solution)/shard_map/ppermute | solution.py:16
  151.3 12.3 %all-to-all-start.1 = ((f32[2,256,256]{2,0,1:T(2,128)}), f32[2,256,256]{2,0,1:T(2,128)S(1)}, u32[]{:S(2)}, u32[]{:S(2)}) async-start(f32[2,256,256]{2,0,1:T(2,128)} %copy.141), calls=%async_computation.1 | async-start | bytes 1048576 | tf_op jit(solution)/shard_map/all_to_all | solution.py:97
  154.8 3.2 %copy-start.1 = (bf16[4,256,1280]{1,2,0:T(8,128)(2,1)S(1)}, bf16[4,256,1280]{1,2,0:T(8,128)(2,1)}, u32[]{:S(2)}) copy-start(bf16[4,256,1280]{1,2,0:T(8,128)(2,1)} %copy-done) | copy-start | bytes 7864324
  166.9 13.5 %all-to-all-start.2 = ((f32[2,4,16,1024]{3,2,0,1:T(8,128)}), f32[2,4,16,1024]{3,2,0,1:T(8,128)S(1)}, u32[]{:S(2)}, u32[]{:S(2)}) async-start(f32[2,4,16,1024]{3,2,0,1:T(8,128)} %copy.144), calls=%async_computation.2 | async-start | bytes 1048576 | tf_op jit(solution)/shard_map/all_to_all | solution.py:101
  171.2 1.6 copy-start.13
  171.2 1.6 copy-start.14
where the time goes:
time: 195 us; the launch traced here: 194 us
  waiting for transfers between devices  60.1 us (31%)
  matrix products  46.9 us (24%)
  starting transfers between devices  38.4 us (20%)
  local copies, waits for them, and re-layouts  24.2 us (12%)
  blocking collectives  12.8 us (7%)
  other arithmetic  10.2 us (5%)
    ppermute x8, waiting for transfers between devices, shifted(): return lax.ppermute(value, axis, pairs)  44.8 us
    ppermute x8, starting transfers between devices, shifted(): return lax.ppermute(value, axis, pairs)  27.3 us
    sub x4, matrix products, head_grads(): weights = jnp.exp(masked - highest)  20.6 us
    unnamed x62, local copies, waits for them, and re-layouts  17.8 us
    all_gather x1, blocking collectives, body(): d_shared_kv = lax.all_gather(chunk, 'section', axis=1, tiled=True)  12.8 us
    convert_element_type x4, other arithmetic, head_grads(): probs_b = probs.astype(jnp.bfloat16)  8.43 us
    dot_general x4, matrix products, head_grads(): jnp.einsum('gre,ed->rgd', dscores_b, keys_head, preferred_element_type=jn...  7.58 us
    all_to_all x1, waiting for transfers between devices, body(): pieces = lax.all_to_all(pieces, 'section', split_axis=1, concat_axis=1)  6.01 us
  transfers between devices with their start and end apart: 11, of which 8 were waited for; matrix products, arithmetic and copies ran while one was open for 10% of the time, Pallas kernels for 0%

commit v1 on v0

--- a/solution.py
+++ b/solution.py
@@ -8,6 +8,19 @@
 KVH = 8
 HD = 128
 WINDOW = 1024
+
+
+def gather_around(x, axis, dim):
+    ways = lax.axis_size(axis)
+    up = [(d, (d + 1) % ways) for d in range(ways)]
+    down = [(d, (d - 1) % ways) for d in range(ways)]
+    earlier, later = ([x], [x])
+    for _ in range(ways // 2):
+        earlier.append(lax.ppermute(earlier[-1], axis, up))
+    for _ in range((ways - 1) // 2):
+        later.append(lax.ppermute(later[-1], axis, down))
+    line = jnp.concatenate([*earlier[::-1], *later[1:]], axis=dim)
+    return jnp.roll(line, (lax.axis_index(axis) - ways // 2) * x.shape[dim], axis=dim)
 
 
 def shifted(value, axis, by):
@@ -102,7 +115,7 @@
     chunk = pieces[:, 0]
     for other in range(1, sections):
         chunk = chunk + pieces[:, other]
-    d_shared_kv = lax.all_gather(chunk, "section", axis=1, tiled=True)
+    d_shared_kv = gather_around(chunk, "section", 1)
     return (d_queries, d_shared_kv)
 
 

time: 195 us -> 198 us (1.015)
  blocking collectives: 12.8 us -> 0 us
  waiting for transfers between devices: 60.1 us -> 68 us
  starting transfers between devices: 38.4 us -> 42.3 us
    all_gather x1 -> x0, blocking collectives: 12.8 us -> none  [body(): d_shared_kv = lax.all_gather(chunk, 'section', axis=1, tiled=True)]
    ppermute x0 -> x3, waiting for transfers between devices: none -> 6.54 us  [the longest x2 5.46 us: gather_around(): earlier.append(lax.ppermute(earlier[-1], axis, up))]
    ppermute x0 -> x3, starting transfers between devices: none -> 3.86 us  [the longest x1 3.21 us: gather_around(): later.append(lax.ppermute(later[-1], axis, down))]
    all_to_all x1, waiting for transfers between devices: 3.31 us -> 6.35 us  [body(): lax.all_to_all(own_rows, 'tp', split_axis=1, concat_axis=2, tiled=True)]
    all_to_all x1, waiting for transfers between devices: 6.01 us -> 3.73 us  [body(): pieces = lax.all_to_all(pieces, 'section', split_axis=1, concat_axis=1)]
    unnamed x62 -> x70, local copies, waits for them, and re-layouts: 17.8 us -> 17.7 us
  transfers between devices with their start and end apart: 11 -> 14, of which waited for: 8 -> 11; matrix products, arithmetic and copies ran while one was open for 10% -> 11% of each run, Pallas kernels for 0% -> 0%
where the time goes in v1:
time: 198 us; the launch traced here: 196 us
  waiting for transfers between devices  68 us (34%)
  matrix products  48.8 us (25%)
  starting transfers between devices  42.3 us (21%)
  local copies, waits for them, and re-layouts  24.9 us (13%)
  other arithmetic  10.3 us (5%)
    ppermute x8, waiting for transfers between devices, shifted(): return lax.ppermute(value, axis, pairs)  45.4 us
    ppermute x8, starting transfers between devices, shifted(): return lax.ppermute(value, axis, pairs)  27.3 us
    sub x4, matrix products, head_grads(): weights = jnp.exp(masked - highest)  20.6 us
    unnamed x70, local copies, waits for them, and re-layouts  17.7 us
    dot_general x4, matrix products, head_grads(): jnp.einsum('gre,ed->rgd', dscores_b, keys_head, preferred_element_type=jn...  9.35 us
    convert_element_type x4, other arithmetic, head_grads(): probs_b = probs.astype(jnp.bfloat16)  8.43 us
    all_to_all x1, waiting for transfers between devices, body(): lax.all_to_all(own_rows, 'tp', split_axis=1, concat_axis=2, tiled=True)  6.35 us
    all_to_all x1, waiting for transfers between devices, body(): lax.all_to_all(shared_kv, 'tp', split_axis=2, concat_axis=1, tiled=True)  5.94 us
  transfers between devices with their start and end apart: 14, of which 11 were waited for; matrix products, arithmetic and copies ran while one was open for 11% of the time, Pallas kernels for 0%

profile of v1, /device:TPU:80, one launch (start us, length us, event | category | flops | bytes accessed | tf_op | source)
XLA Modules:
  0.0 195.7 jit_solution(781189364204119263)
XLA Ops:
  0.6 1.4 copy.93
  3.1 3.4 %all-to-all-start = ((bf16[4,2,16384]{2,1,0:T(2,128)(2,1)}), bf16[4,2,16384]{2,1,0:T(2,128)(2,1)S(1)}, u32[]{:S(2)}, u32[]{:S(2)}) async-start(bf16[4,2,16384]{2,1,0:T(2,128)(2,1)} %reshape.113), calls=%async_computation | async-start | bytes 524288 | tf_op jit(solution)/shard_map/all_to_all | solution.py:60
  6.5 5.9 %all-to-all-done = bf16[4,2,16384]{2,1,0:T(2,128)(2,1)S(1)} async-done(((bf16[4,2,16384]{2,1,0:T(2,128)(2,1)}), bf16[4,2,16384]{2,1,0:T(2,128)(2,1)S(1)}, u32[]{:S(2)}, u32[]{:S(2)}) %all-to-all-start) | async-done | bytes 262176 | tf_op jit(solution)/shard_map/all_to_all | solution.py:60
  13.9 6.4 %collective-permute-start = (bf16[2,256,256]{2,1,0:T(8,128)(2,1)}, bf16[2,256,256]{2,1,0:T(8,128)(2,1)}, u32[]{:S(2)}, u32[]{:S(2)}) collective-permute-start(bf16[2,256,256]{2,1,0:T(8,128)(2,1)} %bitcast.2), channel_id=1, source_target_pairs={{0,16},{4,20},{8,24},{12,28},{16,32},{20,36},{24,40},{28,44},{32,4... | collective-permute-start | bytes 786440 | tf_op jit(solution)/shard_map/ppermute | solution.py:29
  20.2 1.1 fusion.28
  21.9 2.9 %collective-permute-start.2 = (bf16[2,256,256]{2,1,0:T(8,128)(2,1)}, bf16[2,256,256]{2,1,0:T(8,128)(2,1)}, u32[]{:S(2)}, u32[]{:S(2)}) collective-permute-start(bf16[2,256,256]{2,1,0:T(8,128)(2,1)} %bitcast.2), channel_id=1, source_target_pairs={{0,8},{4,12},{8,16},{12,20},{16,24},{20,28},{24,32},{28,36},{32,40... | collective-permute-start | bytes 786440 | tf_op jit(solution)/shard_map/ppermute | solution.py:29
  24.8 3.2 %collective-permute-start.1 = (bf16[2,256,256]{2,1,0:T(8,128)(2,1)}, bf16[2,256,256]{2,1,0:T(8,128)(2,1)}, u32[]{:S(2)}, u32[]{:S(2)}) collective-permute-start(bf16[2,256,256]{2,1,0:T(8,128)(2,1)} %bitcast.2), channel_id=1, source_target_pairs={{0,12},{4,16},{8,20},{12,24},{16,28},{20,32},{24,36},{28,40},{32,4... | collective-permute-start | bytes 786440 | tf_op jit(solution)/shard_map/ppermute | solution.py:29
  28.1 1.5 copy.95
  33.1 5.3 %collective-permute-start.3 = (bf16[2,256,256]{2,1,0:T(8,128)(2,1)}, bf16[2,256,256]{2,1,0:T(8,128)(2,1)S(1)}, u32[]{:S(2)}, u32[]{:S(2)}) collective-permute-start(bf16[2,256,256]{2,1,0:T(8,128)(2,1)} %bitcast.2), channel_id=1, source_target_pairs={{0,4},{4,8},{8,12},{12,16},{16,20},{20,24},{24,28},{28,32},{32,36}... | collective-permute-start | bytes 786440 | tf_op jit(solution)/shard_map/ppermute | solution.py:29
  39.4 10.3 %collective-permute-done.1 = bf16[2,256,256]{2,1,0:T(8,128)(2,1)} collective-permute-done((bf16[2,256,256]{2,1,0:T(8,128)(2,1)}, bf16[2,256,256]{2,1,0:T(8,128)(2,1)}, u32[]{:S(2)}, u32[]{:S(2)}) %collective-permute-start.1) | collective-permute-done | bytes 262176 | tf_op jit(solution)/shard_map/ppermute | solution.py:29
  51.6 2.3 %collective-permute-done.3 = bf16[2,256,256]{2,1,0:T(8,128)(2,1)S(1)} collective-permute-done((bf16[2,256,256]{2,1,0:T(8,128)(2,1)}, bf16[2,256,256]{2,1,0:T(8,128)(2,1)S(1)}, u32[]{:S(2)}, u32[]{:S(2)}) %collective-permute-start.3) | collective-permute-done | bytes 262176 | tf_op jit(solution)/shard_map/ppermute | solution.py:29
  54.9 5.3 %exponential_reduce_fusion.3 = (f32[4,256]{1,0:T(4,128)S(1)}, f32[4,256,1280]{1,2,0:T(8,128)}) fusion(pred[256,1280]{0,1:T(8,128)(4,1)} %fusion.28, bf16[256,16,128]{0,2,1:T(8,128)(2,1)S(1)} %bitcast.231, bf16[2,1280,256]{2,1,0:T(8,128)(2,1)S(1)} %constant_dynamic-update-slice_fusion), kind=kOutput, calls=%fused_computation.31 | convolution fusion | flops 340788480 | bytes 6164480 | tf_op jit(solution)/shard_map/sub | solution.py:39
  60.1 5.1 %exponential_reduce_fusion.1 = (f32[4,256]{1,0:T(4,128)S(1)}, f32[4,256,1280]{1,2,0:T(8,128)}) fusion(pred[256,1280]{0,1:T(8,128)(4,1)} %fusion.28, bf16[256,16,128]{0,2,1:T(8,128)(2,1)S(1)} %bitcast.232, bf16[2,1280,256]{2,1,0:T(8,128)(2,1)S(1)} %constant_dynamic-update-slice_fusion), kind=kOutput, calls=%fused_computation.27 | convolution fusion | flops 340788480 | bytes 6164480 | tf_op jit(solution)/shard_map/sub | solution.py:39
  65.3 5.1 %exponential_reduce_fusion.2 = (f32[4,256]{1,0:T(4,128)S(1)}, f32[4,256,1280]{1,2,0:T(8,128)}) fusion(pred[256,1280]{0,1:T(8,128)(4,1)} %fusion.28, bf16[256,16,128]{0,2,1:T(8,128)(2,1)S(1)} %bitcast.233, bf16[2,1280,256]{2,1,0:T(8,128)(2,1)S(1)} %constant_dynamic-update-slice_fusion), kind=kOutput, calls=%fused_computation.29 | convolution fusion | flops 340788480 | bytes 6164480 | tf_op jit(solution)/shard_map/sub | solution.py:39
  70.4 5.1 %exponential_reduce_fusion = (f32[4,256]{1,0:T(4,128)S(1)}, f32[4,256,1280]{1,2,0:T(8,128)}) fusion(pred[256,1280]{0,1:T(8,128)(4,1)} %fusion.28, bf16[256,16,128]{0,2,1:T(8,128)(2,1)S(1)} %bitcast.234, bf16[2,1280,256]{2,1,0:T(8,128)(2,1)S(1)} %constant_dynamic-update-slice_fusion), kind=kOutput, calls=%fused_computation.25 | convolution fusion | flops 340788480 | bytes 6164480 | tf_op jit(solution)/shard_map/sub | solution.py:39
  75.5 4.0 %fusion.23 = bf16[4,256,1280]{1,2,0:T(8,128)(2,1)S(1)} fusion(f32[4,256]{1,0:T(4,128)S(1)} %get-tuple-element.22, f32[4,256,1280]{1,2,0:T(8,128)} %get-tuple-element.23), kind=kLoop, calls=%fused_computation.50 | loop fusion | flops 2621440 | bytes 7868416 | tf_op jit(solution)/shard_map/convert_element_type | solution.py:41
  80.5 1.3 fusion.37
  81.8 1.1 fusion.15
  85.2 1.6 fusion.25
  87.8 1.3 fusion.39
  89.1 1.1 fusion.11
  92.6 1.4 fusion.24
  94.0 1.3 fusion.38
  96.3 1.1 fusion.13
  97.4 1.2 slice-done
  99.7 1.4 fusion.26
  101.1 1.3 fusion.40
  103.4 2.5 %fusion.9 = bf16[4,256,1280]{1,2,0:T(8,128)(2,1)S(1)} fusion(f32[4,256]{1,0:T(4,128)S(1)} %bitcast.243, f32[4,256]{1,0:T(4,128)S(1)} %get-tuple-element.16, f32[4,256,1280]{1,2,0:T(8,128)S(1)} %bitcast.224, bf16[2,1280,256]{2,1,0:T(8,128)(2,1)} %copy-done.5, bf16[256,16,128]{0,2,1:T(8,128)(2,1)} %bitcast.222), kind=kOutput, calls=%fused_computation.10 | convolution fusion | flops 340787200 | bytes 8462336 | tf_op jit(solution)/shard_map/rgd,ed->gre/dot_general | solution.py:44
  108.4 1.9 collective-permute-start.4
  110.4 3.8 %collective-permute-start.7 = (bf16[2,256,256]{1,2,0:T(8,128)(2,1)S(1)}, bf16[2,256,256]{1,2,0:T(8,128)(2,1)S(1)}, u32[]{:S(2)}, u32[]{:S(2)}) collective-permute-start(bf16[2,256,256]{1,2,0:T(8,128)(2,1)S(1)} %get-tuple-element.9), channel_id=1, source_target_pairs={{4,0},{8,4},{12,8},{16,12},{20,16},{24,20},{28,24},{32,28},{36,32}... | collective-permute-start | bytes 786440 | tf_op jit(solution)/shard_map/ppermute | solution.py:29
  114.1 1.9 collective-permute-start.6
  116.1 1.9 collective-permute-start.5
  118.0 8.5 %collective-permute-done.4 = bf16[2,256,256]{1,2,0:T(8,128)(2,1)S(1)} collective-permute-done((bf16[2,256,256]{1,2,0:T(8,128)(2,1)S(1)}, bf16[2,256,256]{1,2,0:T(8,128)(2,1)S(1)}, u32[]{:S(2)}, u32[]{:S(2)}) %collective-permute-start.4) | collective-permute-done | bytes 262176 | tf_op jit(solution)/shard_map/ppermute | solution.py:29
  126.5 7.0 %collective-permute-done.7 = bf16[2,256,256]{1,2,0:T(8,128)(2,1)S(1)} collective-permute-done((bf16[2,256,256]{1,2,0:T(8,128)(2,1)S(1)}, bf16[2,256,256]{1,2,0:T(8,128)(2,1)S(1)}, u32[]{:S(2)}, u32[]{:S(2)}) %collective-permute-start.7) | collective-permute-done | bytes 262176 | tf_op jit(solution)/shard_map/ppermute | solution.py:29
  133.6 17.3 %collective-permute-done.5 = bf16[2,256,256]{1,2,0:T(8,128)(2,1)S(1)} collective-permute-done((bf16[2,256,256]{1,2,0:T(8,128)(2,1)S(1)}, bf16[2,256,256]{1,2,0:T(8,128)(2,1)S(1)}, u32[]{:S(2)}, u32[]{:S(2)}) %collective-permute-start.5) | collective-permute-done | bytes 262176 | tf_op jit(solution)/shard_map/ppermute | solution.py:29
  152.0 3.5 %all-to-all-start.1 = ((f32[2,256,256]{2,0,1:T(2,128)}), f32[2,256,256]{2,0,1:T(2,128)S(1)}, u32[]{:S(2)}, u32[]{:S(2)}) async-start(f32[2,256,256]{2,0,1:T(2,128)} %copy.141), calls=%async_computation.1 | async-start | bytes 1048576 | tf_op jit(solution)/shard_map/all_to_all | solution.py:110
  155.5 2.4 %fusion.44 = bf16[256,4,128]{0,2,1:T(8,128)(2,1)S(1)} fusion(bf16[4,256,1280]{1,2,0:T(8,128)(2,1)} %copy-done.3, bf16[2,1280,256]{2,1,0:T(8,128)(2,1)} %copy-done.5), kind=kOutput, calls=%fused_computation.83 | convolution fusion | flops 335806464 | bytes 3211264 | tf_op jit(solution)/shard_map/gre,ed->rgd/dot_general | solution.py:48
  157.9 6.4 %all-to-all-done.1 = f32[2,256,256]{2,0,1:T(2,128)S(1)} async-done(((f32[2,256,256]{2,0,1:T(2,128)}), f32[2,256,256]{2,0,1:T(2,128)S(1)}, u32[]{:S(2)}, u32[]{:S(2)}) %all-to-all-start.1) | async-done | bytes 524320 | tf_op jit(solution)/shard_map/all_to_all | solution.py:110
  165.7 1.9 copy.144
  167.6 4.3 %all-to-all-start.2 = ((f32[2,4,16,1024]{3,2,0,1:T(8,128)}), f32[2,4,16,1024]{3,2,0,1:T(8,128)S(1)}, u32[]{:S(2)}, u32[]{:S(2)}) async-start(f32[2,4,16,1024]{3,2,0,1:T(8,128)} %copy.144), calls=%async_computation.2 | async-start | bytes 1048576 | tf_op jit(solution)/shard_map/all_to_all | solution.py:114
  171.9 3.2 %fusion.42 = bf16[256,4,128]{0,2,1:T(8,128)(2,1)} fusion(bf16[4,256,1280]{1,2,0:T(8,128)(2,1)} %copy-done.2, bf16[2,1280,256]{2,1,0:T(8,128)(2,1)} %copy-done.5), kind=kOutput, calls=%fused_computation.81 | convolution fusion | flops 335806464 | bytes 3211264 | tf_op jit(solution)/shard_map/gre,ed->rgd/dot_general | solution.py:48
  175.1 2.2 %fusion.43 = bf16[256,4,128]{0,2,1:T(8,128)(2,1)} fusion(bf16[4,256,1280]{1,2,0:T(8,128)(2,1)S(1)} %copy-done.1, bf16[2,1280,256]{2,1,0:T(8,128)(2,1)} %copy-done.5), kind=kOutput, calls=%fused_computation.82 | convolution fusion | flops 335806464 | bytes 3211264 | tf_op jit(solution)/shard_map/gre,ed->rgd/dot_general | solution.py:48
  177.4 3.7 %all-to-all-done.2 = f32[2,4,16,1024]{3,2,0,1:T(8,128)S(1)} async-done(((f32[2,4,16,1024]{3,2,0,1:T(8,128)}), f32[2,4,16,1024]{3,2,0,1:T(8,128)S(1)}, u32[]{:S(2)}, u32[]{:S(2)}) %all-to-all-start.2) | async-done | bytes 524320 | tf_op jit(solution)/shard_map/all_to_all | solution.py:114
  181.8 1.5 fusion.41
  183.3 4.1 %collective-permute-done.8 = f32[2,16,1024]{2,1,0:T(8,128)S(1)} collective-permute-done((f32[2,16,1024]{2,1,0:T(8,128)S(1)}, f32[2,16,1024]{2,1,0:T(8,128)S(1)}, u32[]{:S(2)}, u32[]{:S(2)}) %collective-permute-start.8) | collective-permute-done | bytes 131104 | tf_op jit(solution)/shard_map/ppermute | solution.py:19
  187.6 1.4 copy.145
  189.0 3.2 %collective-permute-start.10 = (f32[2,16,1024]{2,1,0:T(8,128)S(1)}, f32[2,16,1024]{2,1,0:T(8,128)S(1)}, u32[]{:S(2)}, u32[]{:S(2)}) collective-permute-start(f32[2,16,1024]{2,1,0:T(8,128)S(1)} %copy-done.16), channel_id=1, source_target_pairs={{0,192},{64,0},{128,64},{192,128},{1,193},{65,1},{129,65},{193,129... | collective-permute-start | bytes 393224 | tf_op jit(solution)/shard_map/ppermute | solution.py:21
  192.2 1.4 collective-permute-done.9
  (103 shorter events, 27.9 us)
Async XLA Ops:
  0.6 20.7 %copy-start.12 = (bf16[1,256,2048]{2,1,0:T(8,128)(2,1)S(1)}, bf16[1,256,2048]{2,1,0:T(8,128)(2,1)}, u32[]{:S(2)}) copy-start(bf16[1,256,2048]{2,1,0:T(8,128)(2,1)} %param.4) | copy-start | bytes 3145732
  3.1 9.4 %all-to-all-start = ((bf16[4,2,16384]{2,1,0:T(2,128)(2,1)}), bf16[4,2,16384]{2,1,0:T(2,128)(2,1)S(1)}, u32[]{:S(2)}, u32[]{:S(2)}) async-start(bf16[4,2,16384]{2,1,0:T(2,128)(2,1)} %reshape.113), calls=%async_computation | async-start | bytes 524288 | tf_op jit(solution)/shard_map/all_to_all | solution.py:60
  13.9 24.5 %collective-permute-start = (bf16[2,256,256]{2,1,0:T(8,128)(2,1)}, bf16[2,256,256]{2,1,0:T(8,128)(2,1)}, u32[]{:S(2)}, u32[]{:S(2)}) collective-permute-start(bf16[2,256,256]{2,1,0:T(8,128)(2,1)} %bitcast.2), channel_id=1, source_target_pairs={{0,16},{4,20},{8,24},{12,28},{16,32},{20,36},{24,40},{28,44},{32,4... | collective-permute-start | bytes 786440 | tf_op jit(solution)/shard_map/ppermute | solution.py:29
  21.9 80.5 %copy-start.4 = (bf16[1,256,2048]{1,2,0:T(8,128)(2,1)}, bf16[1,256,2048]{1,2,0:T(8,128)(2,1)S(1)}, u32[]{:S(2)}) copy-start(bf16[1,256,2048]{1,2,0:T(8,128)(2,1)S(1)} %copy.97) | copy-start | bytes 3145732
  21.9 28.7 %collective-permute-start.2 = (bf16[2,256,256]{2,1,0:T(8,128)(2,1)}, bf16[2,256,256]{2,1,0:T(8,128)(2,1)}, u32[]{:S(2)}, u32[]{:S(2)}) collective-permute-start(bf16[2,256,256]{2,1,0:T(8,128)(2,1)} %bitcast.2), channel_id=1, source_target_pairs={{0,8},{4,12},{8,16},{12,20},{16,24},{20,28},{24,32},{28,36},{32,40... | collective-permute-start | bytes 786440 | tf_op jit(solution)/shard_map/ppermute | solution.py:29
  24.8 24.8 %collective-permute-start.1 = (bf16[2,256,256]{2,1,0:T(8,128)(2,1)}, bf16[2,256,256]{2,1,0:T(8,128)(2,1)}, u32[]{:S(2)}, u32[]{:S(2)}) collective-permute-start(bf16[2,256,256]{2,1,0:T(8,128)(2,1)} %bitcast.2), channel_id=1, source_target_pairs={{0,12},{4,16},{8,20},{12,24},{16,28},{20,32},{24,36},{28,40},{32,4... | collective-permute-start | bytes 786440 | tf_op jit(solution)/shard_map/ppermute | solution.py:29
  29.6 60.7 %copy-start.6 = (bf16[1,256,2048]{1,2,0:T(8,128)(2,1)}, bf16[1,256,2048]{1,2,0:T(8,128)(2,1)S(1)}, u32[]{:S(2)}) copy-start(bf16[1,256,2048]{1,2,0:T(8,128)(2,1)S(1)} %copy.95) | copy-start | bytes 3145732
  33.1 20.8 %collective-permute-start.3 = (bf16[2,256,256]{2,1,0:T(8,128)(2,1)}, bf16[2,256,256]{2,1,0:T(8,128)(2,1)S(1)}, u32[]{:S(2)}, u32[]{:S(2)}) collective-permute-start(bf16[2,256,256]{2,1,0:T(8,128)(2,1)} %bitcast.2), channel_id=1, source_target_pairs={{0,4},{4,8},{8,12},{12,16},{16,20},{20,24},{24,28},{28,32},{32,36}... | collective-permute-start | bytes 786440 | tf_op jit(solution)/shard_map/ppermute | solution.py:29
  54.9 46.2 %copy-start.5 = (bf16[2,1280,256]{2,1,0:T(8,128)(2,1)}, bf16[2,1280,256]{2,1,0:T(8,128)(2,1)S(1)}, u32[]{:S(2)}) copy-start(bf16[2,1280,256]{2,1,0:T(8,128)(2,1)S(1)} %constant_dynamic-update-slice_fusion) | copy-start | bytes 3932164
  75.5 6.3 %slice-start.6 = ((s8[5242880]{0:T(1024)(128)(4,1)}), s8[4194304]{0:T(1024)(128)(4,1)S(1)}, s32[]{:S(2)}) async-start(s8[5242880]{0:T(1024)(128)(4,1)} %bitcast.229), calls=%async_computation.9 | async-start | bytes 8388608
  79.5 1.0 copy-start.11
  79.5 2.3 %slice-start.7 = ((s8[5242880]{0:T(1024)(128)(4,1)}), s8[1048576]{0:T(1024)(128)(4,1)S(1)}, s32[]{:S(2)}) async-start(s8[5242880]{0:T(1024)(128)(4,1)} %bitcast.229), calls=%async_computation.10 | async-start | bytes 2097152
  81.8 2.7 %slice-start.4 = ((s8[5242880]{0:T(1024)(128)(4,1)}), s8[4194304]{0:T(1024)(128)(4,1)S(1)}, s32[]{:S(2)}) async-start(s8[5242880]{0:T(1024)(128)(4,1)} %bitcast.227), calls=%async_computation.7 | async-start | bytes 8388608
  81.8 3.4 %slice-start.5 = ((s8[5242880]{0:T(1024)(128)(4,1)}), s8[1048576]{0:T(1024)(128)(4,1)S(1)}, s32[]{:S(2)}) async-start(s8[5242880]{0:T(1024)(128)(4,1)} %bitcast.227), calls=%async_computation.8 | async-start | bytes 2097152
  83.0 1.5 copy-start.3
  86.8 1.0 copy-start.10
  89.1 2.8 %slice-start.2 = ((s8[5242880]{0:T(1024)(128)(4,1)}), s8[4194304]{0:T(1024)(128)(4,1)S(1)}, s32[]{:S(2)}) async-start(s8[5242880]{0:T(1024)(128)(4,1)} %bitcast.225), calls=%async_computation.5 | async-start | bytes 8388608
  89.1 3.4 %slice-start.3 = ((s8[5242880]{0:T(1024)(128)(4,1)}), s8[1048576]{0:T(1024)(128)(4,1)S(1)}, s32[]{:S(2)}) async-start(s8[5242880]{0:T(1024)(128)(4,1)} %bitcast.225), calls=%async_computation.6 | async-start | bytes 2097152
  90.3 1.6 copy-start.2
  92.5 1.4 copy-start.9
  96.2 2.4 %slice-start = ((s8[5242880]{0:T(1024)(128)(4,1)}), s8[4194304]{0:T(1024)(128)(4,1)S(1)}, s32[]{:S(2)}) async-start(s8[5242880]{0:T(1024)(128)(4,1)} %bitcast.223), calls=%async_computation.3 | async-start | bytes 8388608
  96.3 3.4 %slice-start.1 = ((s8[5242880]{0:T(1024)(128)(4,1)}), s8[1048576]{0:T(1024)(128)(4,1)S(1)}, s32[]{:S(2)}) async-start(s8[5242880]{0:T(1024)(128)(4,1)} %bitcast.223), calls=%async_computation.4 | async-start | bytes 2097152
  97.4 8.5 %copy-start = (bf16[4,256,1280]{1,2,0:T(8,128)(2,1)}, bf16[4,256,1280]{1,2,0:T(8,128)(2,1)S(1)}, u32[]{:S(2)}) copy-start(bf16[4,256,1280]{1,2,0:T(8,128)(2,1)S(1)} %fusion.13) | copy-start | bytes 7864324
  99.7 1.4 copy-start.8
  103.4 2.6 %copy-start.7 = (bf16[1,256,2048]{1,2,0:T(8,128)(2,1)S(1)}, bf16[1,256,2048]{1,2,0:T(8,128)(2,1)}, u32[]{:S(2)}) copy-start(bf16[1,256,2048]{1,2,0:T(8,128)(2,1)} %copy-done.6) | copy-start | bytes 3145732
  108.4 18.1 %collective-permute-start.4 = (bf16[2,256,256]{1,2,0:T(8,128)(2,1)S(1)}, bf16[2,256,256]{1,2,0:T(8,128)(2,1)S(1)}, u32[]{:S(2)}, u32[]{:S(2)}) collective-permute-start(bf16[2,256,256]{1,2,0:T(8,128)(2,1)S(1)} %get-tuple-element.8), channel_id=1, source_target_pairs={{16,0},{20,4},{24,8},{28,12},{32,16},{36,20},{40,24},{44,28},{48,3... | collective-permute-start | bytes 786440 | tf_op jit(solution)/shard_map/ppermute | solution.py:29
  110.4 23.2 %collective-permute-start.7 = (bf16[2,256,256]{1,2,0:T(8,128)(2,1)S(1)}, bf16[2,256,256]{1,2,0:T(8,128)(2,1)S(1)}, u32[]{:S(2)}, u32[]{:S(2)}) collective-permute-start(bf16[2,256,256]{1,2,0:T(8,128)(2,1)S(1)} %get-tuple-element.9), channel_id=1, source_target_pairs={{4,0},{8,4},{12,8},{16,12},{20,16},{24,20},{28,24},{32,28},{36,32}... | collective-permute-start | bytes 786440 | tf_op jit(solution)/shard_map/ppermute | solution.py:29
  114.1 19.4 %collective-permute-start.6 = (bf16[2,256,256]{1,2,0:T(8,128)(2,1)S(1)}, bf16[2,256,256]{1,2,0:T(8,128)(2,1)S(1)}, u32[]{:S(2)}, u32[]{:S(2)}) collective-permute-start(bf16[2,256,256]{1,2,0:T(8,128)(2,1)S(1)} %get-tuple-element.10), channel_id=1, source_target_pairs={{8,0},{12,4},{16,8},{20,12},{24,16},{28,20},{32,24},{36,28},{40,32... | collective-permute-start | bytes 786440 | tf_op jit(solution)/shard_map/ppermute | solution.py:29
  116.1 34.8 %collective-permute-start.5 = (bf16[2,256,256]{1,2,0:T(8,128)(2,1)S(1)}, bf16[2,256,256]{1,2,0:T(8,128)(2,1)S(1)}, u32[]{:S(2)}, u32[]{:S(2)}) collective-permute-start(bf16[2,256,256]{1,2,0:T(8,128)(2,1)S(1)} %get-tuple-element.11), channel_id=1, source_target_pairs={{12,0},{16,4},{20,8},{24,12},{28,16},{32,20},{36,24},{40,28},{44,3... | collective-permute-start | bytes 786440 | tf_op jit(solution)/shard_map/ppermute | solution.py:29
  152.0 12.3 %all-to-all-start.1 = ((f32[2,256,256]{2,0,1:T(2,128)}), f32[2,256,256]{2,0,1:T(2,128)S(1)}, u32[]{:S(2)}, u32[]{:S(2)}) async-start(f32[2,256,256]{2,0,1:T(2,128)} %copy.141), calls=%async_computation.1 | async-start | bytes 1048576 | tf_op jit(solution)/shard_map/all_to_all | solution.py:110
  167.6 13.5 %all-to-all-start.2 = ((f32[2,4,16,1024]{3,2,0,1:T(8,128)}), f32[2,4,16,1024]{3,2,0,1:T(8,128)S(1)}, u32[]{:S(2)}, u32[]{:S(2)}) async-start(f32[2,4,16,1024]{3,2,0,1:T(8,128)} %copy.144), calls=%async_computation.2 | async-start | bytes 1048576 | tf_op jit(solution)/shard_map/all_to_all | solution.py:114
  171.9 3.2 %copy-start.1 = (bf16[4,256,1280]{1,2,0:T(8,128)(2,1)S(1)}, bf16[4,256,1280]{1,2,0:T(8,128)(2,1)}, u32[]{:S(2)}) copy-start(bf16[4,256,1280]{1,2,0:T(8,128)(2,1)} %copy-done) | copy-start | bytes 7864324
  181.1 6.3 %copy-start.13 = (bf16[256,4,128]{0,2,1:T(8,128)(2,1)S(1)}, bf16[256,4,128]{0,2,1:T(8,128)(2,1)}, u32[]{:S(2)}) copy-start(bf16[256,4,128]{0,2,1:T(8,128)(2,1)} %fusion.42) | copy-start | bytes 786436
  181.1 6.3 %copy-start.14 = (bf16[256,4,128]{0,2,1:T(8,128)(2,1)S(1)}, bf16[256,4,128]{0,2,1:T(8,128)(2,1)}, u32[]{:S(2)}) copy-start(bf16[256,4,128]{0,2,1:T(8,128)(2,1)} %fusion.43) | copy-start | bytes 786436
  181.1 6.3 %copy-start.15 = (f32[2,16,1024]{2,1,0:T(8,128)}, f32[2,16,1024]{2,1,0:T(8,128)S(1)}, u32[]{:S(2)}) copy-start(f32[2,16,1024]{2,1,0:T(8,128)S(1)} %fusion.78) | copy-start | bytes 393220
  181.1 6.3 %collective-permute-start.8 = (f32[2,16,1024]{2,1,0:T(8,128)S(1)}, f32[2,16,1024]{2,1,0:T(8,128)S(1)}, u32[]{:S(2)}, u32[]{:S(2)}) collective-permute-start(f32[2,16,1024]{2,1,0:T(8,128)S(1)} %fusion.78), channel_id=1, source_target_pairs={{0,64},{64,128},{128,192},{192,0},{1,65},{65,129},{129,193},{193,1... | collective-permute-start | bytes 393224 | tf_op jit(solution)/shard_map/ppermute | solution.py:19
  187.4 6.2 %collective-permute-start.9 = (f32[2,16,1024]{2,1,0:T(8,128)S(1)}, f32[2,16,1024]{2,1,0:T(8,128)S(1)}, u32[]{:S(2)}, u32[]{:S(2)}) collective-permute-start(f32[2,16,1024]{2,1,0:T(8,128)S(1)} %collective-permute-done.8), channel_id=1, source_target_pairs={{0,64},{64,128},{128,192},{192,0},{1,65},{65,129},{129,193},{193,1... | collective-permute-start | bytes 393224 | tf_op jit(solution)/shard_map/ppermute | solution.py:19
  187.4 1.6 copy-start.16
  189.0 5.7 %collective-permute-start.10 = (f32[2,16,1024]{2,1,0:T(8,128)S(1)}, f32[2,16,1024]{2,1,0:T(8,128)S(1)}, u32[]{:S(2)}, u32[]{:S(2)}) collective-permute-start(f32[2,16,1024]{2,1,0:T(8,128)S(1)} %copy-done.16), channel_id=1, source_target_pairs={{0,192},{64,0},{128,64},{192,128},{1,193},{65,1},{129,65},{193,129... | collective-permute-start | bytes 393224 | tf_op jit(solution)/shard_map/ppermute | solution.py:21
